TPU v7x, 256 devices: a whole 4x4x8 slice. The times are simulated.
256 devices in a mesh: ctx: 16 (over x_lo, z), fsdp: 4 (over y), head: 4 (over x_hi, core).
Axes of the slice: x: 4 (x_hi: 2, x_lo: 2; x = x_hi * 2 + x_lo), y: 4, z: 8, core: 2. Of those that a mesh axis runs over, the one named last changes fastest.
Arguments:
- queries: bfloat16 [4, 8192, 2048], P('fsdp', 'ctx', 'head'), may hold values from -6 to 6
- keys: bfloat16 [4, 8192, 2048], P('fsdp', 'ctx', 'head'), may hold values from -6 to 6
- values: bfloat16 [4, 8192, 2048], P('fsdp', 'ctx', 'head'), may hold values from -6 to 6
- gate_pre: bfloat16 [4, 8192, 2048], P('fsdp', 'ctx', 'head'), may hold values from -6 to 6
- log_decay: float32 [4, 8192, 16], P('fsdp', 'ctx', 'head'), may hold values from -2 to 0, as said below
- out_grad: bfloat16 [4, 8192, 4096], P('fsdp', 'ctx', 'head'), may hold values from -6 to 6
- out_weight: float32 [4096, 2048], P(('ctx', 'fsdp'), 'head'), may hold values from -0.125 to 0.125
- moment_one: float32 [4096, 2048], P(('ctx', 'fsdp'), 'head'), may hold values from -2 to 2
- moment_two: float32 [4096, 2048], P(('ctx', 'fsdp'), 'head'), may hold values from 0.05 to 1
- group_ids: int32 [128], P(('ctx', 'fsdp')), may hold values from 0 to 2
- step_count: int32 [1], replicated, may hold values from 1 to 40
Outputs:
- query_grad: bfloat16 [4, 8192, 2048], P('fsdp', 'ctx', 'head')
- key_grad: bfloat16 [4, 8192, 2048], P('fsdp', 'ctx', 'head')
- value_grad: bfloat16 [4, 8192, 2048], P('fsdp', 'ctx', 'head')
- new_moment_one: float32 [4096, 2048], P(('ctx', 'fsdp'), 'head')
- new_moment_two: float32 [4096, 2048], P(('ctx', 'fsdp'), 'head')
- weight_step: float32 [4096, 2048], P(('ctx', 'fsdp'), 'head')
Inputs may be any that keep to these rules, and one draw needn't show every extreme that they name: `log_decay`: Log-decays per token and head, never positive. `group_ids`: 0 for a frozen block of rows, 1 for one updated without weight decay, 2 for one updated with it.
All inputs are finite; a program needn't handle non-finite values.
Results may differ from a plain program's by a relative error of at most 0.017.
Values may be sent and summed in bfloat16 or wider, within the bound.
No kernel may reach another device: no remote copies, remote signals or barrier semaphores. Data moves between devices by JAX's collectives and lax.ppermute only.
A program may use at most 128 MiB of HBM per device.

v0:
```python
import jax
import jax.numpy as jnp
from jax import lax
from jax.sharding import PartitionSpec as P

HEAD_DIM = 128
SPAN = 256
ROW_BLOCK = 32
NORM_EPS = 1e-06
BETA_ONE = 0.9
BETA_TWO = 0.95
ADAM_EPS = 1e-08
WEIGHT_DECAY = 0.1


def entering(array, axis, combine, identity):
    peers, place = (lax.axis_size(axis), lax.axis_index(axis))
    everything = jax.tree.map(lambda part: lax.all_gather(part, axis), array)
    start = jax.tree.map(
        lambda part, zero: jnp.broadcast_to(jnp.asarray(zero, part.dtype), part.shape),
        array,
        identity,
    )

    def hop(k, before):
        reached = k < place
        new = combine(before, jax.tree.map(lambda part: part[k], everything))
        return jax.tree.map(lambda a, b: jnp.where(reached, a, b), new, before)

    return lax.fori_loop(0, peers, hop, start)


def entering_2(array, axis, join, neutral):
    count = lax.axis_size(axis)
    place = lax.axis_index(axis)
    ahead = count - 1 - place
    gathered = jax.tree.map(
        lambda a, kind: lax.all_gather(a.astype(kind), axis), array, (jnp.bfloat16, jnp.bfloat16)
    )
    state = jax.tree.map(lambda a, e: jnp.zeros_like(a) + jnp.asarray(e, a.dtype), array, neutral)

    def one(hop, state):
        source = count - 1 - hop
        return join(
            state,
            jax.tree.map(
                lambda a, own: lax.dynamic_index_in_dim(a, source, 0, False).astype(own.dtype),
                gathered,
                array,
            ),
        )

    return lax.fori_loop(0, ahead, one, state)


def decay_mask(cumul):
    along = jnp.swapaxes(cumul, 1, 2)
    spread = along[:, :, :, None] - along[:, :, None, :]
    length = cumul.shape[1]
    lower = jnp.tril(jnp.ones((length, length), jnp.float32))
    return jnp.exp(jnp.minimum(spread, 0.0)) * lower


def forward_join(earlier, later):
    return (earlier[0] * later[0], later[0][:, None, None] * earlier[1] + later[1])


def backward_join(earlier, later):
    return (earlier[0] * later[0], later[1] + later[0][:, None, None] * earlier[1])


def per_device(
    queries,
    keys,
    values,
    gate_pre,
    log_decay,
    out_grad,
    out_weight,
    moment_one,
    moment_two,
    group_ids,
    step_count,
):
    tok_local = queries.shape[1]
    head_local = log_decay.shape[2]
    width_local = queries.shape[2]
    blocks = tok_local // SPAN
    shaped = (blocks, SPAN, head_local, HEAD_DIM)
    query_c = queries.reshape(shaped)
    key_c = keys.reshape(shaped)
    value_c = values.reshape(shaped)
    cumul = jnp.cumsum(log_decay.reshape(blocks, SPAN, head_local), axis=1)
    totals = cumul[:, -1, :]
    masking = decay_mask(cumul)
    decay_in = jnp.exp(cumul)[..., None]
    decay_out = jnp.exp(totals[:, None, :] - cumul)[..., None]
    scores = jnp.einsum("cthe,cuhe->chtu", query_c, key_c, preferred_element_type=jnp.float32)
    probs = (scores * masking).astype(jnp.bfloat16)
    intra = jnp.einsum("chtu,cuhe->cthe", probs, value_c, preferred_element_type=jnp.float32)
    scaled = (decay_out * key_c).astype(jnp.bfloat16)
    updates = jnp.einsum("cthe,cthf->chef", scaled, value_c, preferred_element_type=jnp.float32)
    running = jnp.zeros((head_local, HEAD_DIM, HEAD_DIM), jnp.float32)
    leading = jnp.zeros((head_local,), jnp.float32)
    start_list = []
    lead_list = []
    for block in range(blocks):
        start_list.append(running)
        lead_list.append(leading)
        running = jnp.exp(totals[block])[:, None, None] * running + updates[block]
        leading = leading + totals[block]
    local_start = jnp.stack(start_list)
    lead_sums = jnp.stack(lead_list)
    empty_state = jnp.zeros((head_local, HEAD_DIM, HEAD_DIM), jnp.float32)
    ones_gain = jnp.ones((head_local,), jnp.float32)
    _, incoming = entering(
        (jnp.exp(leading), running), "ctx", forward_join, (ones_gain, empty_state)
    )
    states = local_start + jnp.exp(lead_sums)[:, :, None, None] * incoming[None]
    rounded = states.astype(jnp.bfloat16)
    inter = decay_in * jnp.einsum(
        "cthe,chef->cthf", query_c, rounded, preferred_element_type=jnp.float32
    )
    attn = intra + inter
    square = jnp.mean(attn * attn, axis=-1, keepdims=True)
    inverse = lax.rsqrt(square + NORM_EPS)
    normed = attn * inverse
    silu_gate = jax.nn.silu(gate_pre.reshape(shaped).astype(jnp.float32))
    mixed = (normed * silu_gate).astype(jnp.bfloat16).reshape(tok_local, width_local)
    features = lax.all_gather(out_grad, "head", axis=2, tiled=True)[0]
    weight_b = out_weight.astype(jnp.bfloat16)
    columns = features
    mixed_grad = jnp.dot(
        columns,
        lax.all_gather(weight_b, ("ctx", "fsdp"), axis=0, tiled=True),
        preferred_element_type=jnp.float32,
    )
    columns = features
    grad_rows = lax.psum_scatter(
        jnp.einsum("td,th->dh", columns, mixed, preferred_element_type=jnp.float32),
        ("ctx", "fsdp"),
        scatter_dimension=0,
        tiled=True,
    )
    normed_grad = mixed_grad.reshape(shaped) * silu_gate
    inner = jnp.mean(normed_grad * normed, axis=-1, keepdims=True)
    attn_grad = (inverse * (normed_grad - normed * inner)).astype(jnp.bfloat16)
    inners = jnp.einsum("cthf,cuhf->chtu", attn_grad, value_c, preferred_element_type=jnp.float32)
    dprobs = (inners * masking).astype(jnp.bfloat16)
    qgrad = jnp.einsum("chtu,cuhe->cthe", dprobs, key_c, preferred_element_type=jnp.float32)
    kgrad = jnp.einsum("chtu,cthe->cuhe", dprobs, query_c, preferred_element_type=jnp.float32)
    vgrad = jnp.einsum("chtu,cthf->cuhf", probs, attn_grad, preferred_element_type=jnp.float32)
    weighted = (decay_in * query_c).astype(jnp.bfloat16)
    back_updates = jnp.einsum(
        "cthe,cthf->chef", weighted, attn_grad, preferred_element_type=jnp.float32
    )
    backing = jnp.zeros((head_local, HEAD_DIM, HEAD_DIM), jnp.float32)
    trailing = jnp.zeros((head_local,), jnp.float32)
    after_list = [None] * blocks
    trail_list = [None] * blocks
    for block in reversed(range(blocks)):
        after_list[block] = backing
        trail_list[block] = trailing
        backing = jnp.exp(totals[block])[:, None, None] * backing + back_updates[block]
        trailing = trailing + totals[block]
    local_after = jnp.stack(after_list)
    trail_sums = jnp.stack(trail_list)
    _, arriving = entering_2(
        (jnp.exp(leading), backing), "ctx", backward_join, (ones_gain, empty_state)
    )
    after_full = local_after + jnp.exp(trail_sums)[:, :, None, None] * arriving[None]
    back_b = after_full.astype(jnp.bfloat16)
    qgrad = qgrad + decay_in * jnp.einsum(
        "cthf,chef->cthe", attn_grad, rounded, preferred_element_type=jnp.float32
    )
    kgrad = kgrad + decay_out * jnp.einsum(
        "cuhf,chef->cuhe", value_c, back_b, preferred_element_type=jnp.float32
    )
    vgrad = vgrad + decay_out * jnp.einsum(
        "cuhe,chef->cuhf", key_c, back_b, preferred_element_type=jnp.float32
    )
    query_grad = qgrad.astype(jnp.bfloat16).reshape(1, tok_local, width_local)
    key_grad = kgrad.astype(jnp.bfloat16).reshape(1, tok_local, width_local)
    value_grad = vgrad.astype(jnp.bfloat16).reshape(1, tok_local, width_local)
    token_count = tok_local * lax.axis_size("ctx") * lax.axis_size("fsdp")
    grad = grad_rows / jnp.sqrt(jnp.float32(token_count))
    row_group = jnp.repeat(group_ids, ROW_BLOCK)[:, None]
    stepped = step_count[0].astype(jnp.float32)
    first = BETA_ONE * moment_one + (1.0 - BETA_ONE) * grad
    second = BETA_TWO * moment_two + (1.0 - BETA_TWO) * grad * grad
    correct_one = 1.0 - jnp.power(BETA_ONE, stepped)
    correct_two = 1.0 - jnp.power(BETA_TWO, stepped)
    active = row_group >= 1
    decayed = (row_group == 2).astype(jnp.float32)
    direction = (
        first / correct_one / (jnp.sqrt(second / correct_two) + ADAM_EPS)
        + WEIGHT_DECAY * decayed * out_weight
    )
    new_moment_one = jnp.where(active, first, moment_one)
    new_moment_two = jnp.where(active, second, moment_two)
    weight_step = jnp.where(active, direction, 0.0)
    return (query_grad, key_grad, value_grad, new_moment_one, new_moment_two, weight_step)


def solution(mesh):
    in_specs = (
        P("fsdp", "ctx", "head"),
        P("fsdp", "ctx", "head"),
        P("fsdp", "ctx", "head"),
        P("fsdp", "ctx", "head"),
        P("fsdp", "ctx", "head"),
        P("fsdp", "ctx", "head"),
        P(("ctx", "fsdp"), "head"),
        P(("ctx", "fsdp"), "head"),
        P(("ctx", "fsdp"), "head"),
        P(("ctx", "fsdp")),
        P(),
    )
    out_specs = (
        P("fsdp", "ctx", "head"),
        P("fsdp", "ctx", "head"),
        P("fsdp", "ctx", "head"),
        P(("ctx", "fsdp"), "head"),
        P(("ctx", "fsdp"), "head"),
        P(("ctx", "fsdp"), "head"),
    )
    return jax.shard_map(
        per_device, mesh=mesh, in_specs=in_specs, out_specs=out_specs, check_vma=False
    )
```

profile of v0, /device:TPU:4, one launch (start us, length us, event | category | flops | bytes accessed | tf_op | source)
XLA Modules:
  0.0 863.6 jit_solution(1575633204360036188)
XLA Ops:
  8.0 2.4 reduce-window.6
  11.7 1.2 reshape.193
  12.9 1.2 reshape.197
  14.2 1.0 fusion.13
  20.6 2.3 reshape.204
  23.0 2.6 copy.210
  25.6 36.0 %all-gather = f32[16,1,4]{2,1,0:T(1,128)S(1)} all-gather(f32[1,1,4]{2,1,0:T(1,128)S(1)} %get-tuple-element.320), channel_id=1, replica_groups=mesh['ctx'=16,'fsdp'=4,'head'=4] {'ctx'}, dimensions={0}, use_global_device_ids=true | all-gather | bytes 272 | tf_op jit(solution)/shard_map/all_gather | solution.py:18
  61.6 33.4 %all-gather.7.cloned.1.call-done = f32[16,4,128,128]{3,2,1,0:T(8,128)} async-done(((f32[1,4,128,128]{3,2,1,0:T(8,128)}), f32[16,4,128,128]{3,2,1,0:T(8,128)}) %all-gather.7.cloned.1.call-update) | async-done | bytes 4194320 | tf_op jit(solution)/shard_map/all_gather | solution.py:18
  95.0 17.5 %while.29 = (s32[]{:T(128)}, f32[4,128,128]{2,1,0:T(8,128)S(1)}, s32[]{:T(128)}, f32[16,4]{1,0:T(8,128)S(1)}, f32[16,4,128,128]{3,2,1,0:T(8,128)}, /*index=5*/s32[]{:T(128)}, s32[]{:T(128)}) while((s32[]{:T(128)}, f32[4,128,128]{2,1,0:T(8,128)S(1)}, s32[]{:T(128)}, f32[16,4]{1,0:T(8,128)S(1)}, f32[16,4,128,128]{3,2,1,0:T(8,128)}, ...), condition=%wide.region_3.4_spmd.clone, body=%wide.region_2.3_spmd.clone.sunk | while | flops 262148 | bytes 786593 | solution.py:30
  95.0 1.0 fusion.50
  96.1 1.1 fusion.50
  97.2 1.1 fusion.50
  98.3 1.1 fusion.50
  99.4 1.1 fusion.50
  100.5 1.1 fusion.50
  101.6 1.1 fusion.50
  102.7 1.1 fusion.50
  103.8 1.1 fusion.50
  104.9 1.1 fusion.50
  106.0 1.1 fusion.50
  107.1 1.1 fusion.50
  108.2 1.1 fusion.50
  109.3 1.1 fusion.50
  110.4 1.1 fusion.50
  111.5 1.1 fusion.50
  112.6 1.4 multiply_reduce_fusion.1
  114.0 283.4 %all-gather.11.cloned.1.call-done = bf16[4096,512]{1,0:T(8,128)(2,1)} async-done(((bf16[64,512]{1,0:T(8,128)(2,1)}), bf16[4096,512]{1,0:T(8,128)(2,1)}) %all-gather.11.cloned.1.call-update) | async-done | bytes 4194320 | tf_op jit(solution)/shard_map/all_gather | solution.py:135
  397.5 6.5 copy.208
  403.9 31.7 %all-gather.9.cloned.1.call-done = bf16[1,512,4096]{2,1,0:T(8,128)(2,1)} async-done(((bf16[1,512,1024]{2,1,0:T(8,128)(2,1)}), bf16[1,512,4096]{2,1,0:T(8,128)(2,1)}) %all-gather.9.cloned.1.call-update) | async-done | bytes 4194320 | tf_op jit(solution)/shard_map/all_gather | solution.py:130
  435.6 6.3 multiply_reduce_fusion
  442.0 1.9 multiply_convert_fusion.2
  444.2 0.8 fusion.27
  445.4 7.8 convolution_bitcast_fusion
  453.2 9.1 %copy.254 = f32[4096,512]{1,0:T(8,128)} copy(f32[4096,512]{0,1:T(8,128)} %convolution_bitcast_fusion) | data formatting | bytes 16777216
  463.2 34.7 %all-gather.1 = bf16[16,1,4]{2,1,0:T(2,128)(2,1)S(1)} all-gather(bf16[1,1,4]{2,1,0:T(2,128)(2,1)S(1)} %copy-done.25), channel_id=1, replica_groups=mesh['ctx'=16,'fsdp'=4,'head'=4] {'ctx'}, dimensions={0}, use_global_device_ids=true | all-gather | bytes 136 | tf_op jit(solution)/shard_map/all_gather | solution.py:38
  499.0 0.9 copy.234
  500.9 1.7 multiply_convert_fusion
  503.5 1.1 fusion.10
  504.7 2.1 copy.216
  506.8 2.0 reshape.198
  508.8 1.6 convolution_bitcast_fusion.6
  510.4 1.7 convolution_bitcast_fusion.5
  512.1 6.4 all-gather.13.cloned.1.call-done
  518.5 15.9 %while.28 = (s32[]{:T(128)}, f32[4,128,128]{2,1,0:T(8,128)S(1)}, s32[]{:T(128)}, bf16[16,4,128,128]{3,2,1,0:T(8,128)(2,1)}, bf16[16,4]{1,0:T(8,128)(2,1)S(1)}, /*index=5*/s32[]{:T(128)}, s32[]{:T(128)}, s32[]{:T(128)}, s32[]{:T(128)}) while((s32[]{:T(128)}, f32[4,128,128]{2,1,0:T(8,128)S(1)}, s32[]{:T(128)}, ...), condition=%wide.region_7.8_spmd, body=%wide.region_6.7_spmd.sunk | while | flops 196618 | bytes 655555 | solution.py:53
  518.5 1.0 convert_add_fusion.2
  519.6 1.0 convert_add_fusion.2
  520.6 1.0 convert_add_fusion.2
  521.7 1.0 convert_add_fusion.2
  522.8 1.0 convert_add_fusion.2
  523.8 1.0 convert_add_fusion.2
  524.9 1.0 convert_add_fusion.2
  525.9 1.0 convert_add_fusion.2
  527.0 1.0 convert_add_fusion.2
  528.1 1.0 convert_add_fusion.2
  529.1 1.0 convert_add_fusion.2
  530.2 1.0 convert_add_fusion.2
  531.2 1.0 convert_add_fusion.2
  532.3 1.0 convert_add_fusion.2
  533.4 1.0 convert_add_fusion.2
  534.4 1.6 fusion.11
  536.4 1.0 reshape.199
  538.3 1.0 reshape.200
  539.2 314.2 %reduce-scatter.4.cloned.1.call-done = f32[64,512]{1,0:T(8,128)} async-done(((f32[4096,512]{1,0:T(8,128)}), f32[64,512]{1,0:T(8,128)}) %reduce-scatter.4.cloned.1.call-update) | async-done | bytes 131088
  853.5 1.0 copy.255
  (150 shorter events, 15.4 us)
Async XLA Ops:
  7.2 87.9 %all-gather.7.cloned.1.call-start = ((), (), s32[]{:S(2)}) async-start(), calls=%async_computation.1 | async-start | bytes 4456448 | tf_op jit(solution)/shard_map/all_gather | solution.py:18
  10.8 7.3 copy-start.15
  11.7 4.3 copy-start.19
  11.7 4.3 copy-start.21
  12.9 3.2 copy-start.10
  14.2 3.5 copy-start.11
  16.1 96.5 %copy-start.3 = (f32[1,4,128,128]{3,2,1,0:T(8,128)}, f32[1,4,128,128]{3,2,1,0:T(8,128)S(1)}, u32[]{:S(2)}) copy-start(f32[1,4,128,128]{3,2,1,0:T(8,128)S(1)} %get-tuple-element.311) | copy-start | bytes 786436
  16.1 381.4 %all-gather.11.cloned.1.call-start = ((), (), s32[]{:S(2)}) async-start(), calls=%async_computation.3 | async-start | bytes 4259840 | tf_op jit(solution)/shard_map/all_gather | solution.py:135
  16.9 418.8 %all-gather.9.cloned.1.call-start = ((), (), s32[]{:S(2)}) async-start(), calls=%async_computation.2 | async-start | bytes 5242880 | tf_op jit(solution)/shard_map/all_gather | solution.py:130
  17.6 500.9 %all-gather.13.cloned.1.call-start = ((), (), s32[]{:S(2)}) async-start(), calls=%async_computation.4 | async-start | bytes 2228224 | tf_op jit(solution)/shard_map/all_gather | solution.py:38
  17.7 1.1 copy-start.12
  18.8 1.3 copy-start
  18.8 0.6 copy-start.23
  18.8 0.7 copy-start.26
  18.8 1.2 copy-start.20
  19.3 42.3 %copy-start.27 = (f32[4]{0:T(128)S(1)}, f32[4]{0:T(128)}, u32[]{:S(2)}) copy-start(f32[4]{0:T(128)} %get-tuple-element.286) | copy-start | bytes 52
  61.6 52.4 %copy-start.17 = (f32[2,4]{1,0:T(2,128)}, f32[2,4]{1,0:T(2,128)S(1)}, u32[]{:S(2)}) copy-start(f32[2,4]{1,0:T(2,128)S(1)} %pad_exponential_fusion.1) | copy-start | bytes 100
  114.0 321.6 %copy-start.16 = (f32[2,256,4]{1,2,0:T(4,128)}, f32[2,256,4]{1,2,0:T(4,128)S(1)}, u32[]{:S(2)}) copy-start(f32[2,256,4]{1,2,0:T(4,128)S(1)} %add_rsqrt_fusion) | copy-start | bytes 24580
  397.5 38.2 %copy-start.1 = (f32[2,256,4,128]{1,3,2,0:T(8,128)S(1)}, f32[2,256,4,128]{1,3,2,0:T(8,128)}, u32[]{:S(2)}) copy-start(f32[2,256,4,128]{1,3,2,0:T(8,128)} %copy.210) | copy-start | bytes 3145732
  435.6 6.3 copy-start.2
  442.0 2.3 copy-start.22
  442.0 2.3 copy-start.28
  443.9 1.2 copy-start.6
  445.1 408.4 %reduce-scatter.4.cloned.1.call-start = ((), (), s32[]{:S(2)}) async-start(), calls=%async_computation.5 | async-start | bytes 8519680
  462.3 0.9 copy-start.25
  462.3 35.8 %copy-start.13 = (f32[64,512]{1,0:T(8,128)S(1)}, f32[64,512]{1,0:T(8,128)}, u32[]{:S(2)}) copy-start(f32[64,512]{1,0:T(8,128)} %param.22) | copy-start | bytes 393220
  462.3 36.7 %copy-start.14 = (f32[64,512]{1,0:T(8,128)S(1)}, f32[64,512]{1,0:T(8,128)}, u32[]{:S(2)}) copy-start(f32[64,512]{1,0:T(8,128)} %param.23) | copy-start | bytes 393220
  462.3 37.5 %copy-start.29 = (s32[2]{0:T(128)S(1)}, s32[2]{0:T(128)}, u32[]{:S(2)}) copy-start(s32[2]{0:T(128)} %param.24) | copy-start | bytes 28
  462.3 38.6 %copy-start.24 = (f32[4]{0:T(128)S(1)}, f32[4]{0:T(128)}, u32[]{:S(2)}) copy-start(f32[4]{0:T(128)} %get-tuple-element.285) | copy-start | bytes 52
  502.6 1.0 copy-start.4
  502.6 0.9 copy-start.18
  512.1 22.3 %copy-start.5 = (f32[1,4,128,128]{3,2,1,0:T(8,128)S(1)}, f32[1,4,128,128]{3,2,1,0:T(8,128)}, u32[]{:S(2)}) copy-start(f32[1,4,128,128]{3,2,1,0:T(8,128)} %get-tuple-element.309) | copy-start | bytes 786436
  537.4 317.0 %copy-start.7 = (f32[64,512]{0,1:T(8,128)S(1)}, f32[64,512]{0,1:T(8,128)}, u32[]{:S(2)}) copy-start(f32[64,512]{0,1:T(8,128)} %copy.236) | copy-start | bytes 393220
  537.4 317.1 %copy-start.8 = (f32[64,512]{0,1:T(8,128)S(1)}, f32[64,512]{0,1:T(8,128)}, u32[]{:S(2)}) copy-start(f32[64,512]{0,1:T(8,128)} %copy.231) | copy-start | bytes 393220
  537.4 317.1 %copy-start.9 = (f32[64,512]{0,1:T(8,128)S(1)}, f32[64,512]{0,1:T(8,128)}, u32[]{:S(2)}) copy-start(f32[64,512]{0,1:T(8,128)} %copy.234) | copy-start | bytes 393220
Sparse Core Ops, SparseCore 0:
  16.2 78.7 all-gather.6
  97.4 300.0 all-gather.10
  399.3 36.2 all-gather.8
  445.2 73.1 all-gather.12
  520.8 332.5 reduce-scatter.3
where the time goes:
time: 865 us; the launch traced here: 864 us
  waiting for transfers between devices  670 us (77%)
  blocking collectives  70.8 us (8%)
  other arithmetic  40.5 us (5%)
  local copies, waits for them, and re-layouts  39.7 us (5%)
  matrix products  26.6 us (3%)
  between operations  15 us (2%)
    unnamed x6, waiting for transfers between devices  315 us
    all_gather x1, waiting for transfers between devices, per_device(): lax.all_gather(weight_b, ('ctx', 'fsdp'), axis=0, tiled=True)  283 us
    all_gather x1, blocking collectives, entering(): everything = jax.tree.map(lambda part: lax.all_gather(part, axis), array)  36 us
    all_gather x1, blocking collectives, entering_2(): lax.all_gather(a.astype(kind), axis)  34.7 us
    all_gather x1, waiting for transfers between devices, entering(): everything = jax.tree.map(lambda part: lax.all_gather(part, axis), array)  33.4 us
    all_gather x1, waiting for transfers between devices, per_device(): features = lax.all_gather(out_grad, 'head', axis=2, tiled=True)[0]  31.7 us
  transfers between devices with their start and end apart: 5, of which 5 were waited for; matrix products, arithmetic and copies ran while one was open for 10% of the time, Pallas kernels for 0%

commit v1 on v0

--- a/solution.py
+++ b/solution.py
@@ -132,7 +132,12 @@
     columns = features
     mixed_grad = jnp.dot(
         columns,
-        lax.all_gather(weight_b, ("ctx", "fsdp"), axis=0, tiled=True),
+        jnp.concatenate(
+            lax.all_to_all(
+                jnp.stack([weight_b] * lax.axis_size(("ctx", "fsdp"))), ("ctx", "fsdp"), 0, 0
+            ),
+            axis=0,
+        ),
         preferred_element_type=jnp.float32,
     )
     columns = features

time: 865 us -> 637 us (0.74)
  waiting for transfers between devices: 670 us -> 321 us
  blocking collectives: 70.8 us -> 178 us
  starting transfers between devices: 0.2 us -> 13.3 us
    all_gather x1 -> x0, waiting for transfers between devices: 283 us -> none  [per_device(): lax.all_gather(weight_b, ('ctx', 'fsdp'), axis=0, tiled=True)]
    all_gather x1, blocking collectives: 36 us -> 148 us  [entering(): everything = jax.tree.map(lambda part: lax.all_gather(part, axis), array)]
    all_gather x1, waiting for transfers between devices: 33.4 us -> 0.02 us  [entering(): everything = jax.tree.map(lambda part: lax.all_gather(part, axis), array)]
    all_gather x1, waiting for transfers between devices: 31.7 us -> 0.01 us  [per_device(): features = lax.all_gather(out_grad, 'head', axis=2, tiled=True)[0]]
    all_to_all x0 -> x1, starting transfers between devices: none -> 13.1 us  [per_device(): lax.all_to_all(jnp.stack([weight_b] * lax.axis_size(('ctx', 'fsdp'))), ('...]
    unnamed x6 -> x5, waiting for transfers between devices: 315 us -> 315 us
  transfers between devices with their start and end apart: 5 -> 5, of which waited for: 5 -> 2; matrix products, arithmetic and copies ran while one was open for 10% -> 13% of each run, Pallas kernels for 0% -> 0%
where the time goes in v1:
time: 637 us; the launch traced here: 635 us
  waiting for transfers between devices  321 us (50%)
  blocking collectives  178 us (28%)
  local copies, waits for them, and re-layouts  41.9 us (7%)
  other arithmetic  40 us (6%)
  matrix products  25.3 us (4%)
  between operations  15 us (2%)
  starting transfers between devices  13.3 us (2%)
    unnamed x5, waiting for transfers between devices  315 us
    all_gather x1, blocking collectives, entering(): everything = jax.tree.map(lambda part: lax.all_gather(part, axis), array)  148 us
    all_gather x1, blocking collectives, entering_2(): lax.all_gather(a.astype(kind), axis)  29.7 us
    select_n x16, other arithmetic, hop(): return jax.tree.map(lambda a, b: jnp.where(reached, a, b), new, before)  16.9 us
    unnamed x72, local copies, waits for them, and re-layouts  16 us
    add x15, other arithmetic, backward_join(): later[1] + later[0][:, None, None] * earlier[1]  15.3 us
    all_to_all x1, starting transfers between devices, per_device(): lax.all_to_all(jnp.stack([weight_b] * lax.axis_size(('ctx', 'fsdp'))), ('...  13.1 us
  transfers between devices with their start and end apart: 5, of which 2 were waited for; matrix products, arithmetic and copies ran while one was open for 13% of the time, Pallas kernels for 0%

profile of v1, /device:TPU:4, one launch (start us, length us, event | category | flops | bytes accessed | tf_op | source)
XLA Modules:
  0.0 634.8 jit_solution(7822206711690761333)
XLA Ops:
  8.0 2.4 reduce-window.6
  11.3 1.2 reshape.198
  12.4 1.2 reshape.202
  13.7 1.0 fusion.13
  15.6 2.5 stack.12
  18.1 13.1 %all-to-all-start = ((bf16[64,64,512]{2,1,0:T(8,128)(2,1)}), bf16[64,64,512]{2,1,0:T(8,128)(2,1)}, u32[]{:S(2)}, u32[]{:S(2)}) async-start(bf16[64,64,512]{2,1,0:T(8,128)(2,1)} %stack.12), calls=%async_computation | async-start | bytes 8388608 | tf_op jit(solution)/shard_map/all_to_all | solution.py:136
  35.4 2.3 reshape.210
  37.7 2.6 copy.210
  40.3 147.9 %all-gather = f32[16,1,4]{2,1,0:T(1,128)S(1)} all-gather(f32[1,1,4]{2,1,0:T(1,128)S(1)} %copy-done.29), channel_id=1, replica_groups=mesh['ctx'=16,'fsdp'=4,'head'=4] {'ctx'}, dimensions={0}, use_global_device_ids=true | all-gather | bytes 272 | tf_op jit(solution)/shard_map/all_gather | solution.py:18
  188.2 17.6 %while.29 = (s32[]{:T(128)}, f32[4,128,128]{2,1,0:T(8,128)S(1)}, s32[]{:T(128)}, f32[16,4]{1,0:T(8,128)S(1)}, f32[16,4,128,128]{3,2,1,0:T(8,128)}, /*index=5*/s32[]{:T(128)}, s32[]{:T(128)}) while((s32[]{:T(128)}, f32[4,128,128]{2,1,0:T(8,128)S(1)}, s32[]{:T(128)}, f32[16,4]{1,0:T(8,128)S(1)}, f32[16,4,128,128]{3,2,1,0:T(8,128)}, ...), condition=%wide.region_3.4_spmd.clone, body=%wide.region_2.3_spmd.clone.sunk | while | flops 262148 | bytes 786593 | solution.py:30
  188.3 1.1 fusion.50
  189.4 1.1 fusion.50
  190.4 1.1 fusion.50
  191.5 1.1 fusion.50
  192.6 1.1 fusion.50
  193.8 1.1 fusion.50
  194.9 1.1 fusion.50
  196.0 1.1 fusion.50
  197.1 1.1 fusion.50
  198.2 1.1 fusion.50
  199.3 1.1 fusion.50
  200.4 1.1 fusion.50
  201.5 1.1 fusion.50
  202.5 1.1 fusion.50
  203.6 1.1 fusion.50
  204.7 1.1 fusion.50
  205.8 1.4 multiply_reduce_fusion.1
  207.3 6.4 %copy.208 = bf16[512,4096]{1,0:T(8,128)(2,1)} copy(bf16[512,4096]{0,1:T(8,128)(2,1)} %bitcast.13) | data formatting | bytes 8388608 | tf_op jit(solution)/shard_map/dot_general | solution.py:133
  213.7 6.3 multiply_reduce_fusion
  220.1 1.9 multiply_convert_fusion.2
  222.3 0.8 fusion.27
  223.6 7.8 %convolution_bitcast_fusion = f32[4096,512]{0,1:T(8,128)} fusion(bf16[1,512,4096]{2,1,0:T(8,128)(2,1)} %all-gather.8.cloned.1.call-done, bf16[64,8,4,128]{3,2,1,0:T(4,128)(2,1)S(1)} %bitcast.124), kind=kOutput, calls=%fused_computation.5 | convolution fusion | flops 2147483648 | bytes 13107200 | tf_op jit(solution)/shard_map/td,th->dh/dot_general | solution.py:145
  231.3 9.1 %copy.254 = f32[4096,512]{1,0:T(8,128)} copy(f32[4096,512]{0,1:T(8,128)} %convolution_bitcast_fusion) | data formatting | bytes 16777216
  240.5 0.8 copy.236
  241.3 29.7 %all-gather.1 = bf16[16,1,4]{2,1,0:T(2,128)(2,1)S(1)} all-gather(bf16[1,1,4]{2,1,0:T(2,128)(2,1)S(1)} %copy-done.26), channel_id=1, replica_groups=mesh['ctx'=16,'fsdp'=4,'head'=4] {'ctx'}, dimensions={0}, use_global_device_ids=true | all-gather | bytes 136 | tf_op jit(solution)/shard_map/all_gather | solution.py:38
  271.2 0.8 copy.231
  272.1 0.8 copy.234
  274.0 1.7 multiply_convert_fusion
  276.6 1.1 fusion.10
  277.8 2.1 copy.216
  279.8 2.0 reshape.204
  281.9 1.6 convolution_bitcast_fusion.6
  284.0 5.8 all-gather.10.cloned.1.call-done
  289.8 15.9 %while.28 = (s32[]{:T(128)}, f32[4,128,128]{2,1,0:T(8,128)S(1)}, s32[]{:T(128)}, bf16[16,4,128,128]{3,2,1,0:T(8,128)(2,1)}, bf16[16,4]{1,0:T(8,128)(2,1)S(1)}, /*index=5*/s32[]{:T(128)}, s32[]{:T(128)}, s32[]{:T(128)}, s32[]{:T(128)}) while((s32[]{:T(128)}, f32[4,128,128]{2,1,0:T(8,128)S(1)}, s32[]{:T(128)}, ...), condition=%wide.region_7.8_spmd, body=%wide.region_6.7_spmd.sunk | while | flops 196618 | bytes 655555 | solution.py:53
  289.9 1.0 convert_add_fusion.2
  290.9 1.0 convert_add_fusion.2
  292.0 1.0 convert_add_fusion.2
  293.0 1.0 convert_add_fusion.2
  294.1 1.0 convert_add_fusion.2
  295.2 1.0 convert_add_fusion.2
  296.2 1.0 convert_add_fusion.2
  297.3 1.0 convert_add_fusion.2
  298.3 1.0 convert_add_fusion.2
  299.4 1.0 convert_add_fusion.2
  300.5 1.0 convert_add_fusion.2
  301.5 1.0 convert_add_fusion.2
  302.6 1.0 convert_add_fusion.2
  303.7 1.0 convert_add_fusion.2
  304.7 1.0 convert_add_fusion.2
  305.8 1.6 fusion.11
  307.8 1.0 reshape.205
  309.6 1.0 reshape.206
  310.6 314.1 %reduce-scatter.4.cloned.1.call-done = f32[64,512]{1,0:T(8,128)} async-done(((f32[4096,512]{1,0:T(8,128)}), f32[64,512]{1,0:T(8,128)}) %reduce-scatter.4.cloned.1.call-update) | async-done | bytes 131088
  624.7 1.0 copy.255
  (154 shorter events, 13.3 us)
Async XLA Ops:
  7.2 181.0 %all-gather.6.cloned.1.call-start = ((), (), s32[]{:S(2)}) async-start(), calls=%async_computation.2 | async-start | bytes 4456448 | tf_op jit(solution)/shard_map/all_gather | solution.py:18
  10.8 22.3 %copy-start.16 = (f32[2,4,256]{2,1,0:T(4,128)}, f32[2,4,256]{2,1,0:T(4,128)S(1)}, u32[]{:S(2)}) copy-start(f32[2,4,256]{2,1,0:T(4,128)S(1)} %reduce_window_sum.24) | copy-start | bytes 24580
  11.2 4.4 copy-start.20
  11.2 4.4 copy-start.22
  11.2 21.3 %copy-start.24 = (f32[4]{0:T(128)}, f32[4]{0:T(128)S(1)}, u32[]{:S(2)}) copy-start(f32[4]{0:T(128)S(1)} %get-tuple-element.285) | copy-start | bytes 52
  11.3 21.3 %copy-start.27 = (f32[4]{0:T(128)}, f32[4]{0:T(128)S(1)}, u32[]{:S(2)}) copy-start(f32[4]{0:T(128)S(1)} %get-tuple-element.286) | copy-start | bytes 52
  12.4 3.2 copy-start.11
  15.6 190.2 %copy-start.4 = (f32[1,4,128,128]{3,2,1,0:T(8,128)}, f32[1,4,128,128]{3,2,1,0:T(8,128)S(1)}, u32[]{:S(2)}) copy-start(f32[1,4,128,128]{3,2,1,0:T(8,128)S(1)} %get-tuple-element.311) | copy-start | bytes 786436
  18.1 13.9 %copy-start.12 = (bf16[1,512,512]{2,1,0:T(8,128)(2,1)S(1)}, bf16[1,512,512]{2,1,0:T(8,128)(2,1)}, u32[]{:S(2)}) copy-start(bf16[1,512,512]{2,1,0:T(8,128)(2,1)} %param.15) | copy-start | bytes 1572868
  18.1 189.1 %all-to-all-start = ((bf16[64,64,512]{2,1,0:T(8,128)(2,1)}), bf16[64,64,512]{2,1,0:T(8,128)(2,1)}, u32[]{:S(2)}, u32[]{:S(2)}) async-start(bf16[64,64,512]{2,1,0:T(8,128)(2,1)} %stack.12), calls=%async_computation | async-start | bytes 8388608 | tf_op jit(solution)/shard_map/all_to_all | solution.py:136
  31.3 182.4 %all-gather.8.cloned.1.call-start = ((), (), s32[]{:S(2)}) async-start(), calls=%async_computation.3 | async-start | bytes 5242880 | tf_op jit(solution)/shard_map/all_gather | solution.py:130
  32.0 257.8 %all-gather.10.cloned.1.call-start = ((), (), s32[]{:S(2)}) async-start(), calls=%async_computation.4 | async-start | bytes 2228224 | tf_op jit(solution)/shard_map/all_gather | solution.py:38
  32.5 1.8 copy-start.13
  33.8 1.0 copy-start
  33.8 1.0 copy-start.21
  35.4 4.9 copy-start.29
  35.4 152.8 %copy-start.28 = (f32[4]{0:T(128)S(1)}, f32[4]{0:T(128)}, u32[]{:S(2)}) copy-start(f32[4]{0:T(128)} %copy-done.27) | copy-start | bytes 52
  188.2 19.1 %copy-start.18 = (f32[2,4]{1,0:T(2,128)}, f32[2,4]{1,0:T(2,128)S(1)}, u32[]{:S(2)}) copy-start(f32[2,4]{1,0:T(2,128)S(1)} %pad_exponential_fusion.1) | copy-start | bytes 100
  207.3 6.5 %copy-start.17 = (f32[2,256,4]{1,2,0:T(4,128)}, f32[2,256,4]{1,2,0:T(4,128)S(1)}, u32[]{:S(2)}) copy-start(f32[2,256,4]{1,2,0:T(4,128)S(1)} %add_rsqrt_fusion) | copy-start | bytes 24580
  207.3 6.4 %copy-start.2 = (f32[2,256,4,128]{1,3,2,0:T(8,128)S(1)}, f32[2,256,4,128]{1,3,2,0:T(8,128)}, u32[]{:S(2)}) copy-start(f32[2,256,4,128]{1,3,2,0:T(8,128)} %copy.210) | copy-start | bytes 3145732
  213.7 6.3 copy-start.3
  220.1 2.3 copy-start.23
  220.1 2.3 copy-start.30
  222.0 1.2 copy-start.7
  223.2 401.5 %reduce-scatter.4.cloned.1.call-start = ((), (), s32[]{:S(2)}) async-start(), calls=%async_computation.5 | async-start | bytes 8519680
  240.4 0.9 copy-start.26
  240.4 30.8 %copy-start.14 = (f32[64,512]{1,0:T(8,128)S(1)}, f32[64,512]{1,0:T(8,128)}, u32[]{:S(2)}) copy-start(f32[64,512]{1,0:T(8,128)} %param.22) | copy-start | bytes 393220
  240.4 31.6 %copy-start.15 = (f32[64,512]{1,0:T(8,128)S(1)}, f32[64,512]{1,0:T(8,128)}, u32[]{:S(2)}) copy-start(f32[64,512]{1,0:T(8,128)} %param.23) | copy-start | bytes 393220
  240.4 32.5 %copy-start.31 = (s32[2]{0:T(128)S(1)}, s32[2]{0:T(128)}, u32[]{:S(2)}) copy-start(s32[2]{0:T(128)} %param.24) | copy-start | bytes 28
  240.4 33.5 %copy-start.25 = (f32[4]{0:T(128)S(1)}, f32[4]{0:T(128)}, u32[]{:S(2)}) copy-start(f32[4]{0:T(128)} %copy-done.24) | copy-start | bytes 52
  275.7 1.0 copy-start.5
  275.7 0.9 copy-start.19
  281.9 1.6 copy-start.1
  283.9 21.8 %copy-start.6 = (f32[1,4,128,128]{3,2,1,0:T(8,128)S(1)}, f32[1,4,128,128]{3,2,1,0:T(8,128)}, u32[]{:S(2)}) copy-start(f32[1,4,128,128]{3,2,1,0:T(8,128)} %get-tuple-element.309) | copy-start | bytes 786436
  308.8 316.9 %copy-start.8 = (f32[64,512]{0,1:T(8,128)S(1)}, f32[64,512]{0,1:T(8,128)}, u32[]{:S(2)}) copy-start(f32[64,512]{0,1:T(8,128)} %copy.236) | copy-start | bytes 393220
  308.8 316.9 %copy-start.9 = (f32[64,512]{0,1:T(8,128)S(1)}, f32[64,512]{0,1:T(8,128)}, u32[]{:S(2)}) copy-start(f32[64,512]{0,1:T(8,128)} %copy.231) | copy-start | bytes 393220
  308.8 317.0 %copy-start.10 = (f32[64,512]{0,1:T(8,128)S(1)}, f32[64,512]{0,1:T(8,128)}, u32[]{:S(2)}) copy-start(f32[64,512]{0,1:T(8,128)} %copy.234) | copy-start | bytes 393220
Sparse Core Ops, SparseCore 0:
  15.7 151.8 all-gather.5
  169.4 37.5 all-gather.7
  223.3 66.4 all-gather.9
  292.2 332.4 reduce-scatter.3
